TPU v7x, 512 devices: a whole 4x4x16 slice. The times are simulated.
512 devices in a mesh: seq: 8 (over x, core), tp: 16 (over z), req: 4 (over y).
Axes of the slice: x: 4, y: 4, z: 16, core: 2. Of those that a mesh axis runs over, the one named last changes fastest.
Arguments:
- tokens: bfloat16 [32768, 1792], P(('req', 'seq'), 'tp'), parts along dimension 0, may hold values from -6 to 6
- w_in: bfloat16 [1792, 4096], P(None, 'tp'), may hold values from -0.125 to 0.125
- conv_w: float32 [3, 1792], P(None, 'tp'), may hold values from -3 to 3
- head_gain: float32 [1792], P('tp'), may hold values from 0.1 to 1.9
- w_out: bfloat16 [1792, 1792], P('tp'), may hold values from -0.125 to 0.125
- prompt_lens: int32 [16], P('req'), parts along dimension 0, may hold values from 1 to 4096, 8192 in all
- req_group: int32 [128], P('req'), parts along dimension 0, may hold values from 0 to 3, as said below
- row_request: int32 [128], P('req'), parts along dimension 0, may hold values from 0 to 31, each once
Outputs:
- mixed: bfloat16 [32768, 1792], P(('req', 'seq'), 'tp'), parts along dimension 0
- req_state: float32 [128, 16, 273, 112], P(('req', 'seq'), 'tp'), parts along dimension 0
- req_norm: float32 [128, 16, 273], P(('req', 'seq'), 'tp'), parts along dimension 0
- req_edge: bfloat16 [128, 2, 1792], P(('req', 'seq'), None, 'tp'), parts along dimension 0
There are 4 independent parts, one for each index of `req`. A program takes and returns all parts, laid end to end along the dimension named above; an argument that names none is the same for every part. Nothing has to cross between parts.
Inputs may be any that keep to these rules, and one draw needn't show every extreme that they name: `prompt_lens`: the lengths sum to 8192, and the largest is half of 8192. `req_group`: every one of the 4 prompts is shared by at least one request. `row_request`: each request appears once; rows i * 4 to (i + 1) * 4 - 1 lie on index i of seq.
All inputs are finite; a program needn't handle non-finite values.
Results may differ from a plain program's by a relative error of at most 0.019.
Values may be sent and summed in bfloat16 or wider, within the bound.
No kernel may reach another device: no remote copies, remote signals or barrier semaphores. Data moves between devices by JAX's collectives and lax.ppermute only.
A program may use at most 64 MiB of HBM per device.

v0:
```python
import jax
import jax.numpy as jnp
from jax import lax
from jax.sharding import PartitionSpec as P

FEAT = 16
HD = 112
KW = 3
PROMPTS = 4
SLOTS = 4
EPS = 1e-05
HIGH = lax.Precision.HIGHEST


def passed_along(shard, axis, by):
    size = lax.axis_size(axis)
    pairs = [(i, i + by) for i in range(size) if 0 <= i + by < size]
    return lax.ppermute(shard, axis, pairs)


def prefix(shard, axis, combine, identity):
    size, here = (lax.axis_size(axis), lax.axis_index(axis))
    everything = jax.tree.map(
        lambda part, kind: lax.all_gather(part.astype(kind), axis),
        shard,
        (jnp.bfloat16, jnp.bfloat16),
    )
    start = jax.tree.map(
        lambda part, zero: jnp.broadcast_to(jnp.asarray(zero, part.dtype), part.shape),
        shard,
        identity,
    )

    def step(k, before):
        reached = k < here
        new = combine(
            before, jax.tree.map(lambda part, own: part[k].astype(own.dtype), everything, shard)
        )
        return jax.tree.map(lambda a, b: jnp.where(reached, a, b), new, before)

    return lax.fori_loop(0, size, step, start)


def taylor_map(values):
    size = values.shape[-1]
    ones = jnp.ones(values.shape[:-1] + (1,), jnp.float32)
    pairs = (values[..., :, None] * values[..., None, :]).reshape(
        values.shape[:-1] + (size * size,)
    )
    return jnp.concatenate([ones, values, pairs * 0.5**0.5], axis=-1)


def segment_ids(positions, ends):
    return jnp.sum((positions[:, None] >= ends[None, :]).astype(jnp.int32), axis=1)


def chain_combine(earlier, later):
    keep = 1.0 - later[1]
    return (later[0] + keep * earlier[0], jnp.maximum(earlier[1], later[1]))


def local(tokens, w_in, conv_w, head_gain, w_out, prompt_lens, req_group, row_request):
    tok_rows = tokens.shape[0]
    width = 2 * FEAT + 2 * HD
    local_heads = w_in.shape[1] // width
    local_cols = local_heads * HD
    seq_pos = lax.axis_index("seq")
    first_row = seq_pos * tok_rows
    ends = jnp.cumsum(prompt_lens)
    starts = ends - prompt_lens
    positions = first_row + jnp.arange(tok_rows, dtype=jnp.int32)
    seg = segment_ids(positions, ends)
    proj = jnp.dot(
        lax.all_gather(tokens, "tp", axis=1, tiled=True), w_in, preferred_element_type=jnp.float32
    )
    proj = proj.astype(jnp.bfloat16).reshape(tok_rows, local_heads, width)
    gate_pre = proj[:, :, 2 * FEAT + HD :].reshape(tok_rows, local_cols)
    rim = passed_along(gate_pre[tok_rows - (KW - 1) :], "seq", 1)
    extended = jnp.concatenate([rim, gate_pre], 0)
    ext_pos = first_row - (KW - 1) + jnp.arange(tok_rows + KW - 1, dtype=jnp.int32)
    ext_seg = segment_ids(ext_pos, ends)
    gate = jnp.zeros((tok_rows, local_cols), jnp.float32)
    for tap in range(KW):
        low = KW - 1 - tap
        same = (ext_seg[low : low + tok_rows] == seg).astype(jnp.float32)
        gate = (
            gate
            + conv_w[tap][None, :]
            * extended[low : low + tok_rows].astype(jnp.float32)
            * same[:, None]
        )
    qs = proj[:, :, :FEAT].astype(jnp.float32) * FEAT ** (-0.25)
    ks = proj[:, :, FEAT : 2 * FEAT].astype(jnp.float32) * FEAT ** (-0.25)
    values = proj[:, :, 2 * FEAT : 2 * FEAT + HD]
    values_f = values.astype(jnp.float32)
    dots = jnp.einsum("thf,shf->hts", qs, ks, precision=HIGH)
    visible = ((positions[None, :] <= positions[:, None]) & (seg[:, None] == seg[None, :])).astype(
        jnp.float32
    )
    weights = (1.0 + dots + 0.5 * dots * dots) * visible[None]
    numer = jnp.einsum(
        "hts,shd->thd", weights.astype(jnp.bfloat16), values, preferred_element_type=jnp.float32
    )
    phi_q = taylor_map(qs)
    phi_k = taylor_map(ks)
    tail = (seg == seg[-1]).astype(jnp.float32)
    tail_keys = phi_k * tail[:, None, None]
    tail_state = jnp.einsum("thf,thd->hfd", tail_keys, values_f, precision=HIGH)
    restart = jnp.any((starts >= first_row) & (starts < first_row + tok_rows)).astype(jnp.float32)
    identity = (jnp.zeros_like(tail_state), jnp.zeros((), jnp.float32))
    carry_state, reached = prefix((tail_state, restart), "seq", chain_combine, identity)
    seg_before = jnp.sum((first_row - 1 >= ends).astype(jnp.int32))
    carried = ((seg == seg_before) & (first_row > 0)).astype(jnp.float32)
    attended = (
        numer
        + jnp.einsum("thf,hfd->thd", phi_q, carry_state, precision=HIGH) * carried[:, None, None]
    )
    inv_rms = lax.rsqrt(jnp.mean(attended * attended, axis=2, keepdims=True) + EPS)
    gain = head_gain.reshape(local_heads, HD)
    hidden = (
        attended * inv_rms * gain[None] * jax.nn.silu(gate.reshape(tok_rows, local_heads, HD))
    ).astype(jnp.bfloat16)
    hidden = hidden.reshape(tok_rows, local_cols)
    product = lax.dot_general(
        w_out, hidden, (((0,), (1,)), ((), ())), preferred_element_type=jnp.float32
    )
    summed = lax.psum_scatter(
        lax.optimization_barrier(product.astype(jnp.bfloat16))
        .astype(jnp.float32)
        .astype(jnp.bfloat16),
        "tp",
        scatter_dimension=0,
        tiled=True,
    ).astype(jnp.float32)
    mixed = summed.T.astype(jnp.bfloat16)
    prompt_index = jnp.arange(PROMPTS, dtype=jnp.int32)
    onehot = (seg[:, None] == prompt_index[None, :]).astype(jnp.float32)
    contrib_state = jnp.einsum("tg,thf,thd->ghfd", onehot, phi_k, values_f, precision=HIGH)
    contrib_norm = jnp.einsum("tg,thf->ghf", onehot, phi_k, precision=HIGH)
    offsets = jnp.arange(KW - 1, dtype=jnp.int32)
    edge_rows = ends[:, None] - (KW - 1) + offsets[None, :]
    edge_valid = edge_rows >= starts[:, None]
    scale = lax.rsqrt(prompt_lens.astype(jnp.float32))
    match = ((positions[:, None, None] == edge_rows[None]) & edge_valid[None]).astype(jnp.float32)
    contrib_edge = jnp.einsum("tgj,tc->gjc", match, gate_pre.astype(jnp.float32), precision=HIGH)
    all_state, all_norm, all_edge = (
        lax.psum(contrib_state.astype(jnp.bfloat16), "seq").astype(jnp.float32),
        lax.psum(contrib_norm.astype(jnp.bfloat16), "seq").astype(jnp.float32),
        lax.psum(contrib_edge.astype(jnp.bfloat16), "seq").astype(jnp.float32),
    )
    my_requests = lax.dynamic_slice_in_dim(row_request, seq_pos * SLOTS, SLOTS)
    my_groups = jnp.take(req_group, my_requests)
    pick = (my_groups[:, None] == prompt_index[None, :]).astype(jnp.float32)
    req_state = jnp.einsum("sg,ghfd->shfd", pick * scale[None, :], all_state, precision=HIGH)
    req_norm = jnp.einsum("sg,ghf->shf", pick * scale[None, :], all_norm, precision=HIGH)
    req_edge = jnp.einsum("sg,gjc->sjc", pick, all_edge, precision=HIGH).astype(jnp.bfloat16)
    return (mixed, req_state, req_norm, req_edge)


def solution(mesh):
    in_specs = (
        P(("req", "seq"), "tp"),
        P(None, "tp"),
        P(None, "tp"),
        P("tp"),
        P("tp", None),
        P("req"),
        P("req"),
        P("req"),
    )
    out_specs = (
        P(("req", "seq"), "tp"),
        P(("req", "seq"), "tp", None, None),
        P(("req", "seq"), "tp", None),
        P(("req", "seq"), None, "tp"),
    )
    return jax.shard_map(local, mesh=mesh, in_specs=in_specs, out_specs=out_specs, check_vma=False)
```

profile of v0, /device:TPU:8, one launch (start us, length us, event | category | flops | bytes accessed | tf_op | source)
XLA Modules:
  0.0 269.1 jit_solution(10015217603055386801)
XLA Ops:
  8.0 0.8 reduce-window.7
  8.8 1.3 and_reduce_fusion
  11.5 1.3 dynamic-slice
  14.7 1.4 slice_bitcast_fusion.7
  16.1 1.4 fusion.73
  17.5 73.9 %all-gather.4.cloned.1.call-done = bf16[1024,1792]{0,1:T(8,128)(2,1)} async-done(((bf16[1024,112]{0,1:T(8,128)(2,1)}), bf16[1024,1792]{0,1:T(8,128)(2,1)}) %all-gather.4.cloned.1.call-update) | async-done | bytes 3670032 | tf_op jit(solution)/shard_map/all_gather | solution.py:74
  91.4 3.2 %fusion.7 = bf16[1024,1,256]{0,2,1:T(8,128)(2,1)S(1)} fusion(bf16[1024,1792]{0,1:T(8,128)(2,1)} %all-gather.4.cloned.1.call-done, bf16[1792,256]{1,0:T(8,128)(2,1)S(1)} %copy-done), kind=kOutput, calls=%fused_computation.13 | convolution fusion | flops 939786240 | bytes 5111808 | tf_op jit(solution)/shard_map/dot_general | solution.py:73
  94.8 5.8 %fusion.3 = bf16[1024,1024]{1,0:T(8,128)(2,1)} fusion(s32[1024]{0:T(1024)S(1)} %convert_reduce_fusion.1, s32[1024]{0:T(1024)S(1)} %iota_add_fusion.1, bf16[1024,1,256]{0,2,1:T(8,128)(2,1)S(1)} %fusion.7), kind=kOutput, calls=%fused_computation.6 | convolution fusion | flops 210829312 | bytes 2179072 | tf_op jit(solution)/shard_map/thf,shf->hts/dot_general | solution.py:96
  100.6 1.9 collective-permute-start
  102.7 0.8 fusion.34
  103.7 3.0 %fusion.13 = bf16[4,273,112]{2,1,0:T(8,128)(2,1)} fusion(f32[1024,4]{0,1:T(4,128)S(1)} %fusion.67, f32[1024,112]{0,1:T(8,128)S(1)} %get-tuple-element.168, f32[1024,1,256]{0,2,1:T(8,128)S(1)} %bitcast.134, f32[1024,1,16]{0,2,1:T(8,128)S(1)} %get-tuple-element.170, f32[273]{0:T(512)S(1)} %pad.8.clone), kind=kOutput, calls=%fused_computation.19 | convolution fusion | flops 1504011776 | bytes 1834948 | tf_op jit(solution)/shard_map/tg,thf,thd->ghfd/dot_general | solution.py:138
  106.8 0.8 convolution_convert_fusion.3
  107.6 2.1 fusion.31
  109.6 13.7 %all-gather.1 = bf16[8,273,112]{2,1,0:T(8,128)(2,1)S(1)} all-gather(bf16[1,273,112]{2,1,0:T(8,128)(2,1)S(1)} %fusion.31), channel_id=2, replica_groups=mesh['seq'=8,'tp'=16,'req'=4] {'seq'}, dimensions={0}, use_global_device_ids=true | all-gather | bytes 550368 | tf_op jit(solution)/shard_map/all_gather | solution.py:24
  123.3 15.8 %all-reduce.1 = (bf16[8]{0:T(256)(128)(2,1)}, bf16[4,273]{1,0:T(4,128)(2,1)}, bf16[4,2,112]{2,0,1:T(4,128)(2,1)}) all-reduce(bf16[8]{0:T(256)(128)(2,1)} %copy-done.8, bf16[4,273]{1,0:T(4,128)(2,1)S(1)} %fusion.34, bf16[4,2,112]{2,0,1:T(4,128)(2,1)} %convolution_convert_fusion.3), channel_id=1, replica_groups=mesh['seq'=8,'tp'=16,'req'=4] {'seq'}, use_global_device_ids=true, to_apply=%add | all-reduce | flops 1996 | bytes 7984
  139.1 15.5 %while.14 = (s32[]{:T(128)}, f32[1,273,112]{2,1,0:T(8,128)S(1)}, s32[]{:T(128)}, bf16[8,1,273,112]{3,2,1,0:T(8,128)(2,1)S(1)}, bf16[8]{0:T(256)(128)(2,1)}, /*index=5*/s32[]{:T(128)}, f32[1]{0:T(128)}, s32[]{:T(128)}) while((s32[]{:T(128)}, f32[1,273,112]{2,1,0:T(8,128)S(1)}, s32[]{:T(128)}, ...), condition=%wide.region_4.5_spmd.clone, body=%wide.region_3.4_spmd.clone.sunk | while | flops 152885 | bytes 305899 | solution.py:41
  139.1 1.2 dynamic_slice.27
  141.0 1.2 dynamic_slice.27
  143.0 1.2 dynamic_slice.27
  144.9 1.2 dynamic_slice.27
  146.9 1.2 dynamic_slice.27
  148.8 1.2 dynamic_slice.27
  150.8 1.2 dynamic_slice.27
  152.7 1.2 dynamic_slice.27
  154.7 2.5 convolution_bitcast_fusion.2
  157.2 1.2 multiply_reduce_fusion
  158.5 4.2 %fusion.4 = bf16[1792,1024]{0,1:T(8,128)(2,1)} fusion(bf16[112,1792]{1,0:T(8,128)(2,1)S(1)} %copy-done.9, bf16[1024,112]{0,1:T(8,128)(2,1)S(1)} %get-tuple-element.169, f32[1,112,1024]{2,1,0:T(8,128)S(1)} %get-tuple-element.186, bf16[2,112]{0,1:T(8,128)(2,1)} %collective-permute-done, f32[1024]{0:T(1024)S(1)} %get-tuple-element.176, f32[112]{0:T(128)S(1)} %copy-done.6, ...), kind=kOutput, calls=%fused_computation.8 | convolution fusion | flops 415744000 | bytes 4778176 | tf_op jit(solution)/shard_map/dot_general | solution.py:124
  162.6 6.0 %copy.36 = bf16[1792,1024]{1,0:T(8,128)(2,1)} copy(bf16[1792,1024]{0,1:T(8,128)(2,1)} %fusion.4) | data formatting | bytes 7340032
  171.7 7.4 %all-reduce.4.cloned.1.call-done = bf16[4,273,112]{2,1,0:T(8,128)(2,1)} async-done(((bf16[4,273,112]{2,1,0:T(8,128)(2,1)}), bf16[4,273,112]{2,1,0:T(8,128)(2,1)}) %all-reduce.4.cloned.1.call-update) | async-done | bytes 244624 | tf_op jit(solution)/shard_map/psum | solution.py:147
  179.0 1.6 convolution_bitcast_fusion
  180.7 1.4 copy.33
  182.0 80.6 %reduce-scatter.4.cloned.1.call-done = bf16[112,1024]{1,0:T(8,128)(2,1)} async-done(((bf16[1792,1024]{1,0:T(8,128)(2,1)}), bf16[112,1024]{1,0:T(8,128)(2,1)}) %reduce-scatter.4.cloned.1.call-update) | async-done | bytes 229392
  (69 shorter events, 7.7 us)
Async XLA Ops:
  7.2 84.2 %copy-start = (bf16[1792,256]{1,0:T(8,128)(2,1)S(1)}, bf16[1792,256]{1,0:T(8,128)(2,1)}, u32[]{:S(2)}) copy-start(bf16[1792,256]{1,0:T(8,128)(2,1)} %param.11) | copy-start | bytes 2752516
  7.2 84.2 %all-gather.4.cloned.1.call-start = ((), (), s32[]{:S(2)}) async-start(), calls=%async_computation.1 | async-start | bytes 3899392 | tf_op jit(solution)/shard_map/all_gather | solution.py:74
  7.9 171.1 %all-reduce.4.cloned.1.call-start = ((), (), s32[]{:S(2)}) async-start(), calls=%async_computation.2 | async-start | bytes 573440 | tf_op jit(solution)/shard_map/psum | solution.py:147
  13.5 0.5 copy-start.8
  100.6 57.8 %collective-permute-start = (bf16[2,112]{0,1:T(8,128)(2,1)S(1)}, bf16[2,112]{0,1:T(8,128)(2,1)}, u32[]{:S(2)}, u32[]{:S(2)}) collective-permute-start(bf16[2,112]{0,1:T(8,128)(2,1)S(1)} %slice_bitcast_fusion.4), channel_id=1, source_target_pairs={{0,64},{64,128},{128,192},{192,256},{256,320},{320,384},{384,448},... | collective-permute-start | bytes 1352 | tf_op jit(solution)/shard_map/ppermute | solution.py:18
  102.7 1.0 copy-start.2
  106.7 155.9 %reduce-scatter.4.cloned.1.call-start = ((), (), s32[]{:S(2)}) async-start(), calls=%async_computation.3 | async-start | bytes 3899392
  154.6 3.8 %copy-start.5 = (f32[112]{0:T(128)S(1)}, f32[112]{0:T(128)}, u32[]{:S(2)}) copy-start(f32[112]{0:T(128)} %get-tuple-element.180) | copy-start | bytes 1348
  154.6 3.8 %copy-start.6 = (f32[112]{0:T(128)S(1)}, f32[112]{0:T(128)}, u32[]{:S(2)}) copy-start(f32[112]{0:T(128)} %get-tuple-element.181) | copy-start | bytes 1348
  154.7 3.8 %copy-start.7 = (f32[112]{0:T(128)S(1)}, f32[112]{0:T(128)}, u32[]{:S(2)}) copy-start(f32[112]{0:T(128)} %get-tuple-element.182) | copy-start | bytes 1348
  154.7 3.8 %copy-start.9 = (bf16[112,1792]{1,0:T(8,128)(2,1)S(1)}, bf16[112,1792]{1,0:T(8,128)(2,1)}, u32[]{:S(2)}) copy-start(bf16[112,1792]{1,0:T(8,128)(2,1)} %param.14) | copy-start | bytes 1204228
  154.7 3.8 %copy-start.12 = (f32[112]{0:T(128)S(1)}, f32[112]{0:T(128)}, u32[]{:S(2)}) copy-start(f32[112]{0:T(128)} %param.13) | copy-start | bytes 1348
  168.6 0.7 copy-start.4
  168.6 0.7 copy-start.1
  168.6 1.4 copy-start.3
  168.6 1.5 copy-start.11
  168.6 2.2 copy-start.10
Sparse Core Ops, SparseCore 0:
  10.1 81.2 all-gather.3
  106.8 72.1 all-reduce.3
  182.5 80.0 reduce-scatter.3
where the time goes:
time: 270 us; the launch traced here: 269 us
  waiting for transfers between devices  163 us (60%)
  blocking collectives  29.5 us (11%)
  matrix products  25.4 us (9%)
  local copies, waits for them, and re-layouts  24.4 us (9%)
  between operations  14.7 us (5%)
  loops' own time  5.33 us (2%)
  other arithmetic  5.31 us (2%)
    unnamed x4, waiting for transfers between devices  81.3 us
    all_gather x1, waiting for transfers between devices, local(): lax.all_gather(tokens, 'tp', axis=1, tiled=True)  73.9 us
    unnamed x1, blocking collectives  15.8 us
    all_gather x1, blocking collectives, prefix(): lax.all_gather(part.astype(kind), axis)  13.7 us
    unnamed x33, local copies, waits for them, and re-layouts  12 us
    dynamic_slice x8, local copies, waits for them, and re-layouts, step(): part[k].astype(own.dtype)  9.72 us
    psum x1, waiting for transfers between devices, local(): lax.psum(contrib_state.astype(jnp.bfloat16), 'seq').astype(jnp.float32)  7.38 us
    dot_general x1, matrix products, local(): dots = jnp.einsum('thf,shf->hts', qs, ks, precision=HIGH)  5.77 us
  transfers between devices with their start and end apart: 4, of which 3 were waited for; matrix products, arithmetic and copies ran while one was open for 17% of the time, Pallas kernels for 0%

commit v1 on v0

--- a/solution.py
+++ b/solution.py
@@ -144,7 +144,9 @@
     match = ((positions[:, None, None] == edge_rows[None]) & edge_valid[None]).astype(jnp.float32)
     contrib_edge = jnp.einsum("tgj,tc->gjc", match, gate_pre.astype(jnp.float32), precision=HIGH)
     all_state, all_norm, all_edge = (
-        lax.psum(contrib_state.astype(jnp.bfloat16), "seq").astype(jnp.float32),
+        jnp.sum(lax.all_gather(contrib_state.astype(jnp.bfloat16), "seq"), axis=0).astype(
+            jnp.float32
+        ),
         lax.psum(contrib_norm.astype(jnp.bfloat16), "seq").astype(jnp.float32),
         lax.psum(contrib_edge.astype(jnp.bfloat16), "seq").astype(jnp.float32),
     )

time: 270 us -> 256 us (0.948)
  the two profiles are of different devices: /device:TPU:8 before, /device:TPU:6 now
where the time goes in v1:
time: 256 us; the launch traced here: 255 us
  waiting for transfers between devices  141 us (55%)
  blocking collectives  28 us (11%)
  matrix products  25.9 us (10%)
  local copies, waits for them, and re-layouts  20.4 us (8%)
  other arithmetic  17.6 us (7%)
  between operations  14.8 us (6%)
  loops' own time  5.43 us (2%)
    unnamed x4, waiting for transfers between devices  70.8 us
    all_gather x1, waiting for transfers between devices, local(): lax.all_gather(tokens, 'tp', axis=1, tiled=True)  70.4 us
    all_gather x1, blocking collectives, prefix(): lax.all_gather(part.astype(kind), axis)  15.5 us
    unnamed x1, blocking collectives  12.5 us
    unnamed x59, local copies, waits for them, and re-layouts  12.4 us
    select_n x8, other arithmetic, step(): return jax.tree.map(lambda a, b: jnp.where(reached, a, b), new, before)  7.67 us
    another operation x1, loops' own time, prefix(): return lax.fori_loop(0, size, step, start)  5.43 us
  transfers between devices with their start and end apart: 4, of which 2 were waited for; matrix products, arithmetic and copies ran while one was open for 21% of the time, Pallas kernels for 0%

profile of v1, /device:TPU:6, one launch (start us, length us, event | category | flops | bytes accessed | tf_op | source)
XLA Modules:
  0.0 255.3 jit_solution(17072784926352194108)
XLA Ops:
  8.0 0.8 reduce-window.7
  8.8 1.3 and_reduce_fusion
  12.1 1.3 dynamic-slice
  13.9 0.8 dynamic-update-slice
  17.1 1.4 slice_bitcast_fusion.7
  19.1 1.9 fusion.73
  21.1 70.4 %all-gather.6.cloned.1.call-done = bf16[1024,1792]{0,1:T(8,128)(2,1)} async-done(((bf16[1024,112]{0,1:T(8,128)(2,1)}), bf16[1024,1792]{0,1:T(8,128)(2,1)}) %all-gather.6.cloned.1.call-update) | async-done | bytes 3670032 | tf_op jit(solution)/shard_map/all_gather | solution.py:74
  91.4 3.2 %fusion.7 = bf16[1024,1,256]{0,2,1:T(8,128)(2,1)S(1)} fusion(bf16[1024,1792]{0,1:T(8,128)(2,1)} %all-gather.6.cloned.1.call-done, bf16[1792,256]{1,0:T(8,128)(2,1)S(1)} %copy-done), kind=kOutput, calls=%fused_computation.14 | convolution fusion | flops 939786240 | bytes 5111808 | tf_op jit(solution)/shard_map/dot_general | solution.py:73
  95.5 4.8 %fusion.3 = bf16[1024,1024]{1,0:T(8,128)(2,1)S(1)} fusion(s32[1024]{0:T(1024)S(1)} %convert_reduce_fusion.1, s32[1024]{0:T(1024)S(1)} %copy-done.7, bf16[1024,1,256]{0,2,1:T(8,128)(2,1)S(1)} %fusion.7), kind=kOutput, calls=%fused_computation.6 | convolution fusion | flops 210829312 | bytes 2179072 | tf_op jit(solution)/shard_map/thf,shf->hts/dot_general | solution.py:96
  100.3 1.9 collective-permute-start
  102.4 1.4 fusion.34
  103.8 3.0 %fusion.13 = bf16[4,1,273,112]{3,2,1,0:T(8,128)(2,1)} fusion(f32[1024,4]{0,1:T(4,128)S(1)} %copy-done.5, f32[1024,112]{0,1:T(8,128)S(1)} %get-tuple-element.168, f32[1024,1,256]{0,2,1:T(8,128)S(1)} %bitcast.138, f32[1024,1,16]{0,2,1:T(8,128)S(1)} %get-tuple-element.170, f32[273]{0:T(512)S(1)} %copy-done.9), kind=kOutput, calls=%fused_computation.20 | convolution fusion | flops 1504011776 | bytes 1834948 | tf_op jit(solution)/shard_map/tg,thf,thd->ghfd/dot_general | solution.py:138
  106.9 1.7 convolution_convert_fusion.3
  108.6 2.8 %fusion.31 = bf16[1,273,112]{2,1,0:T(8,128)(2,1)} fusion(f32[1024,1,1,1,1,1,256]{0,6,5,4,3,2,1:T(8,128)} %bitcast.139, f32[1024,1,1,1,1,1,16]{0,6,5,4,3,2,1:T(8,128)} %get-tuple-element.173, f32[273]{0:T(512)} %pad.8.clone, f32[1024]{0:T(1024)} %get-tuple-element.179, bf16[1024,1,256]{0,2,1:T(8,128)(2,1)} %copy-done.3), kind=kOutput, calls=%fused_computation.36 | convolution fusion | flops 376587136 | bytes 1410784 | tf_op jit(solution)/shard_map/thf,thd->hfd/dot_general | solution.py:108
  111.4 12.5 %all-reduce.1 = (bf16[8]{0:T(256)(128)(2,1)}, bf16[4,273]{1,0:T(4,128)(2,1)}, bf16[4,2,112]{2,0,1:T(4,128)(2,1)}) all-reduce(bf16[8]{0:T(256)(128)(2,1)} %copy-done.20, bf16[4,273]{1,0:T(4,128)(2,1)S(1)} %copy-done.14, bf16[4,2,112]{2,0,1:T(4,128)(2,1)} %convolution_convert_fusion.3), channel_id=1, replica_groups=mesh['seq'=8,'tp'=16,'req'=4] {'seq'}, use_global_device_ids=true, to_apply=%add | all-reduce | flops 1996 | bytes 7984
  123.9 15.5 %all-gather.2 = bf16[8,273,112]{2,1,0:T(8,128)(2,1)} all-gather(bf16[1,273,112]{2,1,0:T(8,128)(2,1)} %fusion.31), channel_id=2, replica_groups=mesh['seq'=8,'tp'=16,'req'=4] {'seq'}, dimensions={0}, use_global_device_ids=true | all-gather | bytes 550368 | tf_op jit(solution)/shard_map/all_gather | solution.py:24
  139.4 2.5 convolution_bitcast_fusion.2
  142.2 17.8 %while.14 = (s32[]{:T(128)}, f32[1,273,112]{2,1,0:T(8,128)S(1)}, s32[]{:T(128)}, bf16[8,1,273,112]{3,2,1,0:T(8,128)(2,1)}, bf16[8]{0:T(256)(128)(2,1)S(1)}, /*index=5*/s32[]{:T(128)}, f32[1]{0:T(128)}, s32[]{:T(128)}) while((s32[]{:T(128)}, f32[1,273,112]{2,1,0:T(8,128)S(1)}, s32[]{:T(128)}, bf16[8,1,273,112]{3,2,1,0:T(8,128)(2,1)}, ...), condition=%wide.region_4.5_spmd.clone, body=%wide.region_3.4_spmd.clone.sunk | while | flops 152885 | bytes 305899 | solution.py:41
  143.4 1.0 fusion.103
  145.7 1.0 fusion.103
  147.9 1.0 fusion.103
  150.1 1.0 fusion.103
  152.3 1.0 fusion.103
  154.6 1.0 fusion.103
  156.8 1.0 fusion.103
  159.0 1.0 fusion.103
  160.0 1.2 multiply_reduce_fusion
  161.3 4.2 %fusion.4 = bf16[1792,1024]{0,1:T(8,128)(2,1)} fusion(bf16[112,1792]{1,0:T(8,128)(2,1)S(1)} %copy-done.21, bf16[1024,112]{0,1:T(8,128)(2,1)S(1)} %get-tuple-element.169, f32[1,112,1024]{2,1,0:T(8,128)S(1)} %get-tuple-element.186, bf16[2,112]{0,1:T(8,128)(2,1)} %collective-permute-done, f32[1024]{0:T(1024)S(1)} %copy-done.12, f32[112]{0:T(128)S(1)} %copy-done.18, ...), kind=kOutput, calls=%fused_computation.8 | convolution fusion | flops 415744000 | bytes 4778176 | tf_op jit(solution)/shard_map/dot_general | solution.py:124
  165.5 5.9 %copy.36 = bf16[1792,1024]{1,0:T(8,128)(2,1)} copy(bf16[1792,1024]{0,1:T(8,128)(2,1)} %fusion.4) | data formatting | bytes 7340032
  174.5 2.1 bitcast_reduce_fusion
  177.3 1.4 copy.33
  178.7 70.1 %reduce-scatter.4.cloned.1.call-done = bf16[112,1024]{1,0:T(8,128)(2,1)} async-done(((bf16[1792,1024]{1,0:T(8,128)(2,1)}), bf16[112,1024]{1,0:T(8,128)(2,1)}) %reduce-scatter.4.cloned.1.call-update) | async-done | bytes 229392
  (96 shorter events, 15.3 us)
Async XLA Ops:
  7.2 84.3 %copy-start = (bf16[1792,256]{1,0:T(8,128)(2,1)S(1)}, bf16[1792,256]{1,0:T(8,128)(2,1)}, u32[]{:S(2)}) copy-start(bf16[1792,256]{1,0:T(8,128)(2,1)} %param.11) | copy-start | bytes 2752516
  7.2 84.2 %all-gather.6.cloned.1.call-start = ((), (), s32[]{:S(2)}) async-start(), calls=%async_computation.1 | async-start | bytes 3899392 | tf_op jit(solution)/shard_map/all_gather | solution.py:74
  7.9 166.6 %all-gather.8.cloned.1.call-start = ((), (), s32[]{:S(2)}) async-start(), calls=%async_computation.2 | async-start | bytes 2580480 | tf_op jit(solution)/shard_map/all_gather | solution.py:147
  10.8 0.6 copy-start.6
  14.7 0.6 copy-start.20
  91.4 4.1 %copy-start.7 = (s32[1024]{0:T(1024)S(1)}, s32[1024]{0:T(1024)}, u32[]{:S(2)}) copy-start(s32[1024]{0:T(1024)} %copy-done.6) | copy-start | bytes 12292
  94.6 5.7 %copy-start.3 = (bf16[1024,1,256]{0,2,1:T(8,128)(2,1)}, bf16[1024,1,256]{0,2,1:T(8,128)(2,1)S(1)}, u32[]{:S(2)}) copy-start(bf16[1024,1,256]{0,2,1:T(8,128)(2,1)S(1)} %fusion.7) | copy-start | bytes 1572868
  95.5 6.9 %copy-start.9 = (f32[273]{0:T(512)S(1)}, f32[273]{0:T(512)}, u32[]{:S(2)}) copy-start(f32[273]{0:T(512)} %pad.8.clone) | copy-start | bytes 3280
  100.3 3.5 %copy-start.5 = (f32[1024,4]{0,1:T(4,128)S(1)}, f32[1024,4]{0,1:T(4,128)}, u32[]{:S(2)}) copy-start(f32[1024,4]{0,1:T(4,128)} %fusion.67) | copy-start | bytes 49156
  100.3 60.9 %collective-permute-start = (bf16[2,112]{0,1:T(8,128)(2,1)S(1)}, bf16[2,112]{0,1:T(8,128)(2,1)}, u32[]{:S(2)}, u32[]{:S(2)}) collective-permute-start(bf16[2,112]{0,1:T(8,128)(2,1)S(1)} %slice_bitcast_fusion.4), channel_id=1, source_target_pairs={{0,64},{64,128},{128,192},{192,256},{256,320},{320,384},{384,448},... | collective-permute-start | bytes 1352 | tf_op jit(solution)/shard_map/ppermute | solution.py:18
  102.4 1.4 copy-start.4
  103.8 3.1 %copy-start.8 = (s32[1024]{0:T(1024)S(1)}, s32[1024]{0:T(1024)}, u32[]{:S(2)}) copy-start(s32[1024]{0:T(1024)} %copy-done.6) | copy-start | bytes 12292
  106.9 141.9 %reduce-scatter.4.cloned.1.call-start = ((), (), s32[]{:S(2)}) async-start(), calls=%async_computation.3 | async-start | bytes 3899392
  108.6 2.8 %copy-start.14 = (bf16[4,273]{1,0:T(4,128)(2,1)S(1)}, bf16[4,273]{1,0:T(4,128)(2,1)}, u32[]{:S(2)}) copy-start(bf16[4,273]{1,0:T(4,128)(2,1)} %fusion.34) | copy-start | bytes 6556
  139.4 2.7 %copy-start.25 = (bf16[8]{0:T(256)(128)(2,1)S(1)}, bf16[8]{0:T(256)(128)(2,1)}, u32[]{:S(2)}) copy-start(bf16[8]{0:T(256)(128)(2,1)} %get-tuple-element.222) | copy-start | bytes 52
  141.9 18.0 %copy-start.2 = (f32[1,112,1024]{2,1,0:T(8,128)S(1)}, f32[1,112,1024]{2,1,0:T(8,128)}, u32[]{:S(2)}) copy-start(f32[1,112,1024]{2,1,0:T(8,128)} %convolution_bitcast_fusion.2) | copy-start | bytes 1376260
  141.9 18.0 %copy-start.10 = (f32[273]{0:T(512)S(1)}, f32[273]{0:T(512)}, u32[]{:S(2)}) copy-start(f32[273]{0:T(512)} %pad.8.clone) | copy-start | bytes 3280
  142.1 19.2 %copy-start.11 = (f32[1024]{0:T(1024)S(1)}, f32[1024]{0:T(1024)}, u32[]{:S(2)}) copy-start(f32[1024]{0:T(1024)} %get-tuple-element.175) | copy-start | bytes 12292
  142.1 19.2 %copy-start.12 = (f32[1024]{0:T(1024)S(1)}, f32[1024]{0:T(1024)}, u32[]{:S(2)}) copy-start(f32[1024]{0:T(1024)} %get-tuple-element.176) | copy-start | bytes 12292
  142.1 19.2 %copy-start.13 = (f32[1024]{0:T(1024)S(1)}, f32[1024]{0:T(1024)}, u32[]{:S(2)}) copy-start(f32[1024]{0:T(1024)} %get-tuple-element.177) | copy-start | bytes 12292
  142.1 19.2 %copy-start.17 = (f32[112]{0:T(128)S(1)}, f32[112]{0:T(128)}, u32[]{:S(2)}) copy-start(f32[112]{0:T(128)} %get-tuple-element.180) | copy-start | bytes 1348
  142.1 19.2 %copy-start.18 = (f32[112]{0:T(128)S(1)}, f32[112]{0:T(128)}, u32[]{:S(2)}) copy-start(f32[112]{0:T(128)} %get-tuple-element.181) | copy-start | bytes 1348
  142.1 19.2 %copy-start.19 = (f32[112]{0:T(128)S(1)}, f32[112]{0:T(128)}, u32[]{:S(2)}) copy-start(f32[112]{0:T(128)} %get-tuple-element.182) | copy-start | bytes 1348
  142.2 19.2 %copy-start.21 = (bf16[112,1792]{1,0:T(8,128)(2,1)S(1)}, bf16[112,1792]{1,0:T(8,128)(2,1)}, u32[]{:S(2)}) copy-start(bf16[112,1792]{1,0:T(8,128)(2,1)} %param.14) | copy-start | bytes 1204228
  142.2 19.2 %copy-start.24 = (f32[112]{0:T(128)S(1)}, f32[112]{0:T(128)}, u32[]{:S(2)}) copy-start(f32[112]{0:T(128)} %param.13) | copy-start | bytes 1348
  171.5 0.7 copy-start.16
  171.5 0.7 copy-start.1
  171.5 1.4 copy-start.15
  171.5 1.5 copy-start.23
  171.5 2.2 copy-start.22
Sparse Core Ops, SparseCore 0:
  10.1 81.3 all-gather.5
  107.0 30.9 all-gather.7
  171.6 77.0 reduce-scatter.3
